TPU v7x, 256 devices: a whole 4x4x8 slice. The times are simulated.
256 devices in a mesh: seq: 64 (over x, z, core), tensor: 4 (over y).
Axes of the slice: x: 4, y: 4, z: 8, core: 2. Of those that a mesh axis runs over, the one named last changes fastest.
Arguments:
- hidden: bfloat16 [512, 1280], P('seq', 'tensor'), may hold values from -20 to 20
- inward_weight: bfloat16 [1280, 3, 1280], P(None, None, 'tensor'), may hold values from -0.15625 to 0.15625
- output_weight: bfloat16 [1280, 1280], P('tensor'), may hold values from -0.559017 to 0.559017
- score_gain: float32 [1280], P('tensor'), may hold values from 0.5 to 9
- eigen_rate: float32 [1280], replicated, may hold values from 0.1 to 0.6
- lengths: int32 [512], replicated, may hold values from 1 to 16384, as said below
- page_request: int32 [1536], P('seq'), may hold values from 0 to 511, as said below
- page_number: int32 [1536], P('seq'), may hold values from 0 to 128, as said below
- page_cache: bfloat16 [1536, 128, 2, 1280], P('seq', None, None, 'tensor'), may hold values from -6 to 6
Outputs:
- new_hidden: bfloat16 [512, 1280], P('seq', 'tensor')
Inputs may be any that keep to these rules, and one draw needn't show every extreme that they name: `lengths`: exactly 4 requests have more than 256 cached positions; they have more than 16256, one has exactly 16384. Every other request has at most 256, one exactly 256. `page_request`: each page of each request stands in exactly one slot: pages 0 to 1 of every short request, pages 0 to 127 of every long request. The remaining 2 * 4 slots name a long request with page number 128 and hold nothing live. `page_number`: see page_request.
All inputs are finite; a program needn't handle non-finite values.
Results may differ from a plain program's by a relative error of at most 0.012.
The roundings to bfloat16 on the way count: a program that leaves them out, or rounds other values in their place, can miss the bound.
Values may be sent and summed in bfloat16 or wider, within the bound.
No kernel may reach another device: no remote copies, remote signals or barrier semaphores. Data moves between devices by JAX's collectives and lax.ppermute only.
A program may use at most 192 MiB of HBM per device.

v0:
```python
import math
import jax
import jax.numpy as jnp
from jax import lax
from jax.sharding import PartitionSpec as P

HEAD_DIM = 64
epsilon = 1e-06
far_below = -1e30


def merged_2(part, axis, combine):
    gathered = jax.tree.map(lambda a: lax.all_gather(a, axis), part)

    def take(source):
        return jax.tree.map(lambda a: lax.dynamic_index_in_dim(a, source, 0, False), gathered)

    return lax.fori_loop(
        1, lax.axis_size(axis), lambda source, state: combine(state, take(source)), take(0)
    )


def head_norm(values, gain):
    shaped = values.reshape(values.shape[:-1] + (-1, HEAD_DIM))
    normed = shaped / jnp.sqrt(jnp.mean(shaped * shaped, axis=-1, keepdims=True) + epsilon)
    return normed * gain.reshape(-1, HEAD_DIM)


def scale_heads(summed, factor):
    shaped = summed.reshape(summed.shape[:-1] + (factor.shape[-1], -1))
    return (shaped * factor[..., None]).reshape(summed.shape)


def join_parts(first, second):
    first_max, first_total, first_acc = first
    second_max, second_total, second_acc = second
    top = jnp.maximum(first_max, second_max)
    first_factor = jnp.exp(first_max - top)
    second_factor = jnp.exp(second_max - top)
    return (
        top,
        first_total * first_factor + second_total * second_factor,
        scale_heads(first_acc, first_factor) + scale_heads(second_acc, second_factor),
    )


def local(
    hidden,
    inward_weight,
    output_weight,
    score_gain,
    eigen_rate,
    lengths,
    page_request,
    page_number,
    page_cache,
):
    rows, width_local = hidden.shape
    heads_local = width_local // HEAD_DIM
    gathered = lax.all_gather(hidden, "tensor", axis=1, tiled=True)
    projected = jnp.dot(
        gathered,
        inward_weight.reshape(inward_weight.shape[0], -1),
        preferred_element_type=jnp.float32,
    )
    query = head_norm(projected[:, :width_local], score_gain).astype(jnp.bfloat16)
    key_new = head_norm(projected[:, width_local : 2 * width_local], score_gain).astype(
        jnp.bfloat16
    )
    value_own = projected[:, 2 * width_local :].astype(jnp.bfloat16)
    own_score = jnp.sum(
        query.astype(jnp.float32) * key_new.astype(jnp.float32), axis=-1
    ) / math.sqrt(HEAD_DIM)
    all_queries = lax.all_gather(query.reshape(rows, width_local), "seq", axis=0, tiled=True)
    pages, page_len = (page_cache.shape[0], page_cache.shape[1])
    owner_query = all_queries[page_request].reshape(pages, heads_local, HEAD_DIM)
    keys_scaled = head_norm(page_cache[:, :, 0, :].astype(jnp.float32), score_gain).astype(
        jnp.bfloat16
    )
    values_paged = page_cache[:, :, 1, :].reshape(pages, page_len, heads_local, HEAD_DIM)
    scores = jnp.einsum(
        "sphd,shd->shp", keys_scaled, owner_query, preferred_element_type=jnp.float32
    ) / math.sqrt(HEAD_DIM)
    positions = page_number[:, None] * page_len + jnp.arange(page_len, dtype=jnp.int32)[None, :]
    live_mask = positions < lengths[page_request][:, None]
    page_max = jnp.max(jnp.where(live_mask[:, None, :], scores, far_below), axis=-1)
    weights = jnp.where(live_mask[:, None, :], jnp.exp(scores - page_max[..., None]), 0.0).astype(
        jnp.bfloat16
    )
    page_total = jnp.sum(weights.astype(jnp.float32), axis=-1)
    page_acc = jnp.einsum(
        "shp,sphd->shd", weights, values_paged, preferred_element_type=jnp.float32
    ).reshape(pages, width_local)
    requests = lengths.shape[0]
    onehot = page_request[:, None] == jnp.arange(requests, dtype=jnp.int32)[None, :]
    request_max = jnp.max(jnp.where(onehot[:, :, None], page_max[:, None, :], far_below), axis=0)
    factor = jnp.exp(page_max - request_max[page_request])
    selector = onehot.astype(jnp.float32)
    request_total = jnp.dot(selector.T, page_total * factor, precision=lax.Precision.HIGHEST)
    request_acc = jnp.dot(
        selector.T, scale_heads(page_acc, factor), precision=lax.Precision.HIGHEST
    )
    first_row = lax.axis_index("seq") * rows
    merged = merged_2((request_max, request_total, request_acc), "seq", join_parts)
    home_max = lax.dynamic_slice_in_dim(merged[0], first_row, rows, 0)
    home_total = lax.dynamic_slice_in_dim(merged[1], first_row, rows, 0)
    home_acc = lax.dynamic_slice_in_dim(merged[2], first_row, rows, 0)
    final_max = jnp.maximum(home_max, own_score)
    stored_factor = jnp.exp(home_max - final_max)
    own_factor = jnp.exp(own_score - final_max)
    total = home_total * stored_factor + own_factor
    summed = scale_heads(home_acc, stored_factor) + scale_heads(
        value_own.astype(jnp.float32), own_factor
    )
    attended = (
        (summed.reshape(rows, heads_local, HEAD_DIM) / total[..., None])
        .reshape(rows, width_local)
        .astype(jnp.bfloat16)
    )
    partial_out = jnp.dot(attended, output_weight, preferred_element_type=jnp.float32)
    first_col = lax.axis_index("tensor") * width_local
    rate = lax.dynamic_slice_in_dim(eigen_rate, first_col, width_local, 0)
    state = hidden.astype(jnp.float32)
    width = partial_out.shape[1]
    attn_local = lax.psum_scatter(partial_out, "tensor", scatter_dimension=1, tiled=True)
    attn_square = lax.psum(jnp.sum(attn_local * attn_local, axis=-1), "tensor")
    unit = attn_local / jnp.sqrt(attn_square / width + epsilon)[:, None]
    mixed = state + rate * (unit - state)
    mixed_square = lax.psum(jnp.sum(mixed * mixed, axis=-1), "tensor")
    return (mixed / jnp.sqrt(mixed_square / width + epsilon)[:, None]).astype(jnp.bfloat16)


def solution(mesh):
    placed = (
        P("seq", "tensor"),
        P(None, None, "tensor"),
        P("tensor", None),
        P("tensor"),
        P(),
        P(),
        P("seq"),
        P("seq"),
        P("seq", None, None, "tensor"),
    )
    return jax.shard_map(
        local, mesh=mesh, in_specs=placed, out_specs=P("seq", "tensor"), check_vma=False
    )
```

profile of v0, /device:TPU:2, one launch (start us, length us, event | category | flops | bytes accessed | tf_op | source)
XLA Modules:
  0.0 608.3 jit_solution(11876755678239287850)
XLA Ops:
  8.1 12.7 %all-gather.3 = bf16[4,320,8]{1,2,0:T(8,128)(2,1)S(1)} all-gather(bf16[1,320,8]{1,2,0:T(8,128)(2,1)} %bitcast.78), channel_id=1, replica_groups=mesh['seq'=64,'tensor'=4] {'tensor'}, dimensions={0}, use_global_device_ids=true | all-gather | bytes 25600 | tf_op jit(solution)/shard_map/all_gather | solution.py:60
  22.1 50.5 %all_gather.25 = bf16[512,320]{1,0:T(8,128)(2,1)S(1)} all-gather(bf16[8,320]{1,0:T(8,128)(2,1)S(1)} %get-tuple-element.242), channel_id=1, replica_groups=mesh['seq'=64,'tensor'=4] {'seq'}, dimensions={0}, use_global_device_ids=true | all-gather | bytes 332800 | tf_op jit(solution)/shard_map/all_gather | solution.py:74
  73.3 3.7 fusion.24
  85.1 50.0 %all-gather.1 = f32[32768,5]{0,1:T(8,128)S(1)} all-gather(f32[512,5]{0,1:T(8,128)S(1)} %fusion.12), channel_id=3, replica_groups=mesh['seq'=64,'tensor'=4] {'seq'}, dimensions={0}, use_global_device_ids=true | all-gather | bytes 665600 | tf_op jit(solution)/shard_map/all_gather | solution.py:13
  135.1 50.6 %all-gather = f32[32768,5]{0,1:T(8,128)S(1)} all-gather(f32[512,5]{0,1:T(8,128)S(1)} %select_reduce_fusion), channel_id=2, replica_groups=mesh['seq'=64,'tensor'=4] {'seq'}, dimensions={0}, use_global_device_ids=true | all-gather | bytes 665600 | tf_op jit(solution)/shard_map/all_gather | solution.py:13
  187.0 62.2 %all-gather.6.cloned.1.call-done = f32[32768,320]{0,1:T(8,128)} async-done(((f32[512,320]{0,1:T(8,128)}), f32[32768,320]{0,1:T(8,128)}) %all-gather.6.cloned.1.call-update) | async-done | bytes 41943056 | tf_op jit(solution)/shard_map/all_gather | solution.py:13
  249.1 38.8 %copy.54 = f32[40,8,64,512]{3,2,1,0:T(8,128)} copy(f32[40,8,64,512]{3,1,2,0:T(8,128)} %bitcast.71) | data formatting | bytes 83886080
  289.0 265.0 %while.19 = (s32[]{:T(128)}, f32[512,5]{0,1:T(8,128)S(1)}, f32[512,5]{0,1:T(8,128)S(1)}, f32[512,320]{0,1:T(8,128)S(1)}, f32[64,512,5]{1,2,0:T(8,128)}, /*index=...) while((s32[]{:T(128)}, f32[512,5]{0,1:T(8,128)S(1)}, ...), condition=%wide.region_6.7_spmd, body=%wide.region_5.6_spmd.sunk | while | flops 506885 | bytes 3379351 | solution.py:18
  289.8 3.1 constant_dynamic-slice_fusion.2
  298.2 3.1 constant_dynamic-slice_fusion.2
  306.6 3.1 constant_dynamic-slice_fusion.2
  315.0 3.1 constant_dynamic-slice_fusion.2
  323.4 3.1 constant_dynamic-slice_fusion.2
  327.6 3.1 constant_dynamic-slice_fusion.2
  336.1 3.1 constant_dynamic-slice_fusion.2
  344.5 3.1 constant_dynamic-slice_fusion.2
  352.9 3.1 constant_dynamic-slice_fusion.2
  361.3 3.1 constant_dynamic-slice_fusion.2
  369.7 3.1 constant_dynamic-slice_fusion.2
  378.1 3.1 constant_dynamic-slice_fusion.2
  386.5 3.1 constant_dynamic-slice_fusion.2
  394.9 3.1 constant_dynamic-slice_fusion.2
  403.3 3.1 constant_dynamic-slice_fusion.2
  407.5 3.1 constant_dynamic-slice_fusion.2
  416.0 3.1 constant_dynamic-slice_fusion.2
  424.4 3.1 constant_dynamic-slice_fusion.2
  432.8 3.1 constant_dynamic-slice_fusion.2
  441.2 3.1 constant_dynamic-slice_fusion.2
  449.6 3.1 constant_dynamic-slice_fusion.2
  558.5 22.7 %reduce-scatter.4.cloned.1.call-done = f32[320,8]{1,0:T(8,128)} async-done(((f32[1280,8]{1,0:T(8,128)}), f32[320,8]{1,0:T(8,128)}) %reduce-scatter.4.cloned.1.call-update) | async-done | bytes 10256
  583.1 8.3 %psum.14 = f32[8]{0:T(128)S(1)} all-reduce(f32[8]{0:T(128)S(1)} %multiply_reduce_fusion.4), channel_id=1, replica_groups=mesh['seq'=64,'tensor'=4] {'tensor'}, use_global_device_ids=true, to_apply=%region_11.12 | all-reduce | flops 8 | bytes 64 | tf_op jit(solution)/shard_map/psum | solution.py:126
  591.6 9.2 %psum.15 = f32[8]{0:T(128)S(1)} all-reduce(f32[8]{0:T(128)S(1)} %get-tuple-element.232), channel_id=1, replica_groups=mesh['seq'=64,'tensor'=4] {'tensor'}, use_global_device_ids=true, to_apply=%region_13.14 | all-reduce | flops 8 | bytes 64 | tf_op jit(solution)/shard_map/psum | solution.py:129
  (248 shorter events, 218.5 us)
Async XLA Ops:
  6.5 14.3 %copy-start = (bf16[1280,3,320]{0,2,1:T(8,128)(2,1)S(1)}, bf16[1280,3,320]{0,2,1:T(8,128)(2,1)}, u32[]{:S(2)}) copy-start(bf16[1280,3,320]{0,2,1:T(8,128)(2,1)} %param.12) | copy-start | bytes 7372804
  6.5 15.5 %copy-start.5 = (f32[320]{0:T(512)S(1)}, f32[320]{0:T(512)}, u32[]{:S(2)}) copy-start(f32[320]{0:T(512)} %param.14) | copy-start | bytes 3844
  6.5 242.6 %all-gather.6.cloned.1.call-start = ((), (), s32[]{:S(2)}) async-start(), calls=%async_computation.1 | async-start | bytes 42598400 | tf_op jit(solution)/shard_map/all_gather | solution.py:13
  77.0 0.7 copy-start.2
  77.0 1.5 copy-start.7
  79.3 4.1 copy-start.6
  84.7 496.5 %reduce-scatter.4.cloned.1.call-start = ((), (), s32[]{:S(2)}) async-start(), calls=%async_computation.2 | async-start | bytes 819200
  185.6 1.0 copy-start.3
  554.0 37.4 %copy-start.4 = (bf16[8,320]{1,0:T(8,128)(2,1)S(1)}, bf16[8,320]{1,0:T(8,128)(2,1)}, u32[]{:S(2)}) copy-start(bf16[8,320]{1,0:T(8,128)(2,1)} %param.11) | copy-start | bytes 15364
  554.0 47.5 %copy-start.1 = (bf16[1280,3,320]{0,2,1:T(8,128)(2,1)S(1)}, bf16[1280,3,320]{0,2,1:T(8,128)(2,1)}, u32[]{:S(2)}) copy-start(bf16[1280,3,320]{0,2,1:T(8,128)(2,1)} %param.12) | copy-start | bytes 7372804
Sparse Core Ops, SparseCore 0:
  84.8 164.2 all-gather.5
  558.6 22.5 reduce-scatter.3
where the time goes:
time: 615 us; the launch traced here: 608 us
  local copies, waits for them, and re-layouts  249 us (40%)
  blocking collectives  181 us (29%)
  waiting for transfers between devices  84.9 us (14%)
  other arithmetic  69.5 us (11%)
  between operations  13.6 us (2%)
  matrix products  8.17 us (1%)
    dynamic_slice x66, local copies, waits for them, and re-layouts, take(): lax.dynamic_index_in_dim(a, source, 0, False)  199 us
    all_gather x2, blocking collectives, merged_2(): gathered = jax.tree.map(lambda a: lax.all_gather(a, axis), part)  101 us
    all_gather x1, waiting for transfers between devices, merged_2(): gathered = jax.tree.map(lambda a: lax.all_gather(a, axis), part)  62.2 us
    all_gather x1, blocking collectives, local(): lax.all_gather(query.reshape(rows, width_local), 'seq', axis=0, tiled=True)  50.5 us
    add x63, other arithmetic, join_parts(): first_total * first_factor + second_total * second_factor  46.9 us
    unnamed x19, local copies, waits for them, and re-layouts  40.9 us
    unnamed x3, waiting for transfers between devices  22.8 us
    add x63, other arithmetic, join_parts(): scale_heads(first_acc, first_factor)  18.3 us
  transfers between devices with their start and end apart: 2, of which 2 were waited for; matrix products, arithmetic and copies ran while one was open for 0% of the time, Pallas kernels for 0%

commit v1 on v0

--- a/solution.py
+++ b/solution.py
@@ -71,7 +71,12 @@
     own_score = jnp.sum(
         query.astype(jnp.float32) * key_new.astype(jnp.float32), axis=-1
     ) / math.sqrt(HEAD_DIM)
-    all_queries = lax.all_gather(query.reshape(rows, width_local), "seq", axis=0, tiled=True)
+    all_queries = jnp.concatenate(
+        lax.all_to_all(
+            jnp.stack([query.reshape(rows, width_local)] * lax.axis_size("seq")), "seq", 0, 0
+        ),
+        axis=0,
+    )
     pages, page_len = (page_cache.shape[0], page_cache.shape[1])
     owner_query = all_queries[page_request].reshape(pages, heads_local, HEAD_DIM)
     keys_scaled = head_norm(page_cache[:, :, 0, :].astype(jnp.float32), score_gain).astype(

time: 615 us -> 583 us (0.948)
  blocking collectives: 181 us -> 136 us
  starting transfers between devices: 0.04 us -> 12.1 us
    all_gather x1 -> x0, blocking collectives: 50.5 us -> none  [local(): lax.all_gather(query.reshape(rows, width_local), 'seq', axis=0, tiled=True)]
    all_to_all x0 -> x1, starting transfers between devices: none -> 12 us  [local(): lax.all_to_all(jnp.stack([query.reshape(rows, width_local)] * lax.axis_si...]
    all_to_all x0 -> x1, waiting for transfers between devices: none -> 8.62 us  [local(): lax.all_to_all(jnp.stack([query.reshape(rows, width_local)] * lax.axis_si...]
    all_gather x1, waiting for transfers between devices: 62.2 us -> 55.8 us  [merged_2(): gathered = jax.tree.map(lambda a: lax.all_gather(a, axis), part)]
    unnamed x19 -> x17, local copies, waits for them, and re-layouts: 40.9 us -> 39.9 us
  transfers between devices with their start and end apart: 2 -> 3, of which waited for: 2 -> 3; matrix products, arithmetic and copies ran while one was open for 0% -> 1% of each run, Pallas kernels for 0% -> 0%
where the time goes in v1:
time: 583 us; the launch traced here: 576 us
  local copies, waits for them, and re-layouts  250 us (43%)
  blocking collectives  136 us (23%)
  waiting for transfers between devices  87.3 us (15%)
  other arithmetic  68 us (12%)
  between operations  13.6 us (2%)
  starting transfers between devices  12.1 us (2%)
  matrix products  8.15 us (1%)
    dynamic_slice x66, local copies, waits for them, and re-layouts, take(): lax.dynamic_index_in_dim(a, source, 0, False)  200 us
    all_gather x2, blocking collectives, merged_2(): gathered = jax.tree.map(lambda a: lax.all_gather(a, axis), part)  105 us
    all_gather x1, waiting for transfers between devices, merged_2(): gathered = jax.tree.map(lambda a: lax.all_gather(a, axis), part)  55.8 us
    add x63, other arithmetic, join_parts(): first_total * first_factor + second_total * second_factor  46.7 us
    unnamed x17, local copies, waits for them, and re-layouts  39.9 us
    unnamed x3, waiting for transfers between devices  22.9 us
    add x63, other arithmetic, join_parts(): scale_heads(first_acc, first_factor)  18.3 us
    all_gather x1, blocking collectives, local(): gathered = lax.all_gather(hidden, 'tensor', axis=1, tiled=True)  12.8 us
  transfers between devices with their start and end apart: 3, of which 3 were waited for; matrix products, arithmetic and copies ran while one was open for 1% of the time, Pallas kernels for 0%

profile of v1, /device:TPU:2, one launch (start us, length us, event | category | flops | bytes accessed | tf_op | source)
XLA Modules:
  0.0 576.2 jit_solution(13078112070488191125)
XLA Ops:
  6.5 12.8 %all-gather.3 = bf16[4,320,8]{1,2,0:T(8,128)(2,1)S(1)} all-gather(bf16[1,320,8]{1,2,0:T(8,128)(2,1)} %bitcast.79), channel_id=1, replica_groups=mesh['seq'=64,'tensor'=4] {'tensor'}, dimensions={0}, use_global_device_ids=true | all-gather | bytes 25600 | tf_op jit(solution)/shard_map/all_gather | solution.py:60
  21.5 12.0 %all-to-all-start = ((bf16[64,8,320]{2,1,0:T(8,128)(2,1)}), bf16[64,8,320]{2,1,0:T(8,128)(2,1)S(1)}, u32[]{:S(2)}, u32[]{:S(2)}) async-start(bf16[64,8,320]{2,1,0:T(8,128)(2,1)} %stack.3), calls=%async_computation | async-start | bytes 786432 | tf_op jit(solution)/shard_map/all_to_all | solution.py:75
  33.7 3.7 fusion.24
  39.0 8.6 %all-to-all-done = bf16[64,8,320]{2,1,0:T(8,128)(2,1)S(1)} async-done(((bf16[64,8,320]{2,1,0:T(8,128)(2,1)}), bf16[64,8,320]{2,1,0:T(8,128)(2,1)S(1)}, u32[]{:S(2)}, u32[]{:S(2)}) %all-to-all-start) | async-done | bytes 327712 | tf_op jit(solution)/shard_map/all_to_all | solution.py:75
  55.1 49.3 %all-gather.1 = f32[32768,5]{0,1:T(8,128)S(1)} all-gather(f32[512,5]{0,1:T(8,128)S(1)} %fusion.12), channel_id=3, replica_groups=mesh['seq'=64,'tensor'=4] {'seq'}, dimensions={0}, use_global_device_ids=true | all-gather | bytes 665600 | tf_op jit(solution)/shard_map/all_gather | solution.py:13
  104.4 56.1 %all-gather = f32[32768,5]{0,1:T(8,128)} all-gather(f32[512,5]{0,1:T(8,128)S(1)} %select_reduce_fusion), channel_id=2, replica_groups=mesh['seq'=64,'tensor'=4] {'seq'}, dimensions={0}, use_global_device_ids=true | all-gather | bytes 665600 | tf_op jit(solution)/shard_map/all_gather | solution.py:13
  161.2 55.8 %all-gather.6.cloned.1.call-done = f32[32768,320]{0,1:T(8,128)} async-done(((f32[512,320]{0,1:T(8,128)}), f32[32768,320]{0,1:T(8,128)}) %all-gather.6.cloned.1.call-update) | async-done | bytes 41943056 | tf_op jit(solution)/shard_map/all_gather | solution.py:13
  216.9 38.8 %copy.54 = f32[40,8,64,512]{3,2,1,0:T(8,128)} copy(f32[40,8,64,512]{3,1,2,0:T(8,128)} %bitcast.72) | data formatting | bytes 83886080
  256.8 264.8 %while.19 = (s32[]{:T(128)}, f32[512,5]{0,1:T(8,128)S(1)}, f32[512,5]{0,1:T(8,128)S(1)}, f32[512,320]{0,1:T(8,128)S(1)}, f32[64,512,5]{1,2,0:T(8,128)}, /*index=...) while((s32[]{:T(128)}, f32[512,5]{0,1:T(8,128)S(1)}, ...), condition=%wide.region_6.7_spmd, body=%wide.region_5.6_spmd.sunk | while | flops 506885 | bytes 3379351 | solution.py:18
  257.6 3.1 constant_dynamic-slice_fusion.2
  270.2 3.1 constant_dynamic-slice_fusion.2
  274.4 3.1 constant_dynamic-slice_fusion.2
  278.6 3.1 constant_dynamic-slice_fusion.2
  291.2 3.1 constant_dynamic-slice_fusion.2
  295.4 3.1 constant_dynamic-slice_fusion.2
  312.2 3.1 constant_dynamic-slice_fusion.2
  316.5 3.1 constant_dynamic-slice_fusion.2
  329.1 3.1 constant_dynamic-slice_fusion.2
  333.3 3.1 constant_dynamic-slice_fusion.2
  337.5 3.1 constant_dynamic-slice_fusion.2
  350.1 3.1 constant_dynamic-slice_fusion.2
  354.3 3.1 constant_dynamic-slice_fusion.2
  358.5 3.1 constant_dynamic-slice_fusion.2
  371.1 3.1 constant_dynamic-slice_fusion.2
  375.3 3.1 constant_dynamic-slice_fusion.2
  392.1 3.1 constant_dynamic-slice_fusion.2
  396.3 3.1 constant_dynamic-slice_fusion.2
  408.9 3.1 constant_dynamic-slice_fusion.2
  413.1 3.1 constant_dynamic-slice_fusion.2
  526.2 22.9 %reduce-scatter.4.cloned.1.call-done = f32[320,8]{1,0:T(8,128)} async-done(((f32[1280,8]{1,0:T(8,128)}), f32[320,8]{1,0:T(8,128)}) %reduce-scatter.4.cloned.1.call-update) | async-done | bytes 10256
  551.0 8.3 %psum.14 = f32[8]{0:T(128)S(1)} all-reduce(f32[8]{0:T(128)S(1)} %multiply_reduce_fusion.4), channel_id=1, replica_groups=mesh['seq'=64,'tensor'=4] {'tensor'}, use_global_device_ids=true, to_apply=%region_11.12 | all-reduce | flops 8 | bytes 64 | tf_op jit(solution)/shard_map/psum | solution.py:131
  559.5 9.1 %psum.15 = f32[8]{0:T(128)S(1)} all-reduce(f32[8]{0:T(128)S(1)} %get-tuple-element.232), channel_id=1, replica_groups=mesh['seq'=64,'tensor'=4] {'tensor'}, use_global_device_ids=true, to_apply=%region_13.14 | all-reduce | flops 8 | bytes 64 | tf_op jit(solution)/shard_map/psum | solution.py:134
  (248 shorter events, 220.6 us)
Async XLA Ops:
  6.5 12.9 %copy-start = (bf16[1280,3,320]{0,2,1:T(8,128)(2,1)S(1)}, bf16[1280,3,320]{0,2,1:T(8,128)(2,1)}, u32[]{:S(2)}) copy-start(bf16[1280,3,320]{0,2,1:T(8,128)(2,1)} %param.12) | copy-start | bytes 7372804
  6.5 14.0 %copy-start.4 = (f32[320]{0:T(512)S(1)}, f32[320]{0:T(512)}, u32[]{:S(2)}) copy-start(f32[320]{0:T(512)} %param.14) | copy-start | bytes 3844
  6.5 27.1 %copy-start.5 = (s32[24]{0:T(128)S(1)}, s32[24]{0:T(128)}, u32[]{:S(2)}) copy-start(s32[24]{0:T(128)} %param.17) | copy-start | bytes 292
  21.5 26.1 %all-to-all-start = ((bf16[64,8,320]{2,1,0:T(8,128)(2,1)}), bf16[64,8,320]{2,1,0:T(8,128)(2,1)S(1)}, u32[]{:S(2)}, u32[]{:S(2)}) async-start(bf16[64,8,320]{2,1,0:T(8,128)(2,1)} %stack.3), calls=%async_computation | async-start | bytes 786432 | tf_op jit(solution)/shard_map/all_to_all | solution.py:75
  33.5 183.4 %all-gather.6.cloned.1.call-start = ((), (), s32[]{:S(2)}) async-start(), calls=%async_computation.2 | async-start | bytes 42598400 | tf_op jit(solution)/shard_map/all_gather | solution.py:13
  33.7 3.7 copy-start.6
  33.7 3.7 copy-start.2
  54.4 494.6 %reduce-scatter.4.cloned.1.call-start = ((), (), s32[]{:S(2)}) async-start(), calls=%async_computation.3 | async-start | bytes 819200
  521.7 37.6 %copy-start.3 = (bf16[8,320]{1,0:T(8,128)(2,1)S(1)}, bf16[8,320]{1,0:T(8,128)(2,1)}, u32[]{:S(2)}) copy-start(bf16[8,320]{1,0:T(8,128)(2,1)} %param.11) | copy-start | bytes 15364
  521.7 47.6 %copy-start.1 = (bf16[1280,3,320]{0,2,1:T(8,128)(2,1)S(1)}, bf16[1280,3,320]{0,2,1:T(8,128)(2,1)}, u32[]{:S(2)}) copy-start(bf16[1280,3,320]{0,2,1:T(8,128)(2,1)} %param.12) | copy-start | bytes 7372804
Sparse Core Ops, SparseCore 0:
  54.5 162.3 all-gather.5
  526.3 22.7 reduce-scatter.3
